TPU v7x, 256 devices: a whole 4x4x8 slice. The times are simulated.
256 devices in a mesh: blk: 64 (over z, x, core), head: 2 (over y_hi), dec: 2 (over y_lo).
Axes of the slice: x: 4, y: 4 (y_hi: 2, y_lo: 2; y = y_hi * 2 + y_lo), z: 8, core: 2. Of those that a mesh axis runs over, the one named last changes fastest.
Arguments:
- queries: bfloat16 [16384, 1536], P('blk', ('head', 'dec')), may hold values from -12 to 12
- key_vectors: bfloat16 [16384, 1536], P('blk', ('head', 'dec')), may hold values from -5 to 5
- values: bfloat16 [16384, 1536], P('blk', ('head', 'dec')), may hold values from -6 to 6
- lookback: int32 [12], replicated, may hold values from 0 to 5, as said below
- residual: bfloat16 [16384, 3072], P(('blk', 'head', 'dec')), may hold values from -0.1875 to 0.1875
- out_weight: bfloat16 [1536, 3072], P(('head', 'dec')), may hold values from -0.15625 to 0.15625
- branch_gate: float32 [3072], replicated, may hold values from 0.5 to 1.5
- final_shift: float32 [3072], replicated, may hold values from -0.5 to 0.5
- final_scale: float32 [3072], replicated, may hold values from -0.5 to 0.5
- final_weight: bfloat16 [3072, 64], replicated, may hold values from -0.109375 to 0.109375
- decoder_kernel: bfloat16 [432, 512], replicated, may hold values from -0.3125 to 0.3125
- decoder_bias: float32 [512], replicated, may hold values from -3 to 3
Outputs:
- features: bfloat16 [1024, 64, 512], P(('blk', 'head', 'dec'))
Inputs may be any that keep to these rules, and one draw needn't show every extreme that they name: lookback[h] is how many frames before its own the queries of head h may see; some head sees 5 earlier frames and some head none.
All inputs are finite; a program needn't handle non-finite values.
Results may differ from a plain program's by a relative error of at most 0.02.
Values may be sent and summed in bfloat16 or wider, within the bound.
No kernel may reach another device: no remote copies, remote signals or barrier semaphores. Data moves between devices by JAX's collectives and lax.ppermute only.
A program may use at most 192 MiB of HBM per device.

v0:
```python
import jax
import jax.numpy as jnp
from jax import lax
from jax.sharding import PartitionSpec as P

DH = 128
LC = 16
FRAMES = 8
PW = 32


def padded_2(cells, sides, width):
    for axis, dim in sides:
        count = lax.axis_size(axis)
        ends = count - 1
        head = lax.slice_in_dim(cells, 0, width, axis=dim)
        tail = lax.slice_in_dim(cells, cells.shape[dim] - width, cells.shape[dim], axis=dim)
        cells = jnp.concatenate(
            [
                lax.ppermute(tail, axis, [(i, (i + 1) % count) for i in range(ends)]),
                cells,
                lax.ppermute(head, axis, [((i + 1) % count, i) for i in range(ends)]),
            ],
            axis=dim,
        )
    return cells


def from_behind(x, axis, by):
    peers = lax.axis_size(axis)
    pairs = [(i, i + by) for i in range(peers) if 0 <= i + by < peers]
    return lax.ppermute(x, axis, pairs)


def attend_block(carry, shard_pair, query_heads, query_frame, lookback_heads, frame_len):
    running_max, row_total, accumulated = carry
    key_block, value_block = shard_pair
    key_count = key_block.shape[0]
    head_count = query_heads.shape[1]
    key_heads = key_block.reshape(key_count, head_count, DH)
    value_heads = value_block.reshape(key_count, head_count, DH)
    scores = jnp.einsum(
        "qhd,khd->hqk", query_heads, key_heads, preferred_element_type=jnp.float32
    ) * DH ** (-0.5)
    key_pos = jnp.arange(key_count, dtype=jnp.int32)
    key_frame = key_pos // frame_len
    visible = (
        (key_pos >= 0)[None, None, :]
        & (key_frame[None, None, :] <= query_frame[None, :, None])
        & (key_frame[None, None, :] >= query_frame[None, :, None] - lookback_heads[:, None, None])
    )
    masked = jnp.where(visible, scores, -1e30)
    newest_max = jnp.maximum(running_max, jnp.max(masked, axis=2))
    weights = jnp.where(visible, jnp.exp(scores - newest_max[:, :, None]), 0.0).astype(jnp.bfloat16)
    row_total = jnp.sum(weights.astype(jnp.float32), axis=2)
    accumulated = jnp.einsum(
        "hqk,khd->hqd", weights, value_heads, preferred_element_type=jnp.float32
    )
    return (newest_max, row_total, accumulated)


def per_device(
    queries,
    key_vectors,
    values,
    lookback,
    residual,
    out_weight,
    branch_gate,
    final_shift,
    final_scale,
    final_weight,
    decoder_kernel,
    decoder_bias,
):
    slab_rows = queries.shape[0]
    head_count = queries.shape[1] // DH
    blocks = lax.axis_size("blk")
    block_index = lax.axis_index("blk")
    frame_len = slab_rows * blocks // FRAMES
    query_heads = queries.reshape(slab_rows, head_count, DH)
    query_frame = (block_index * slab_rows + jnp.arange(slab_rows, dtype=jnp.int32)) // frame_len
    lookback_heads = lax.dynamic_slice_in_dim(
        lookback, lax.axis_index(("head", "dec")) * head_count, head_count
    )
    initial = (
        jnp.full((head_count, slab_rows), -1e30, jnp.float32),
        jnp.zeros((head_count, slab_rows), jnp.float32),
        jnp.zeros((head_count, slab_rows, DH), jnp.float32),
    )
    carry = attend_block(
        initial,
        (
            lax.all_gather(key_vectors, "blk", axis=0, tiled=True),
            lax.all_gather(values, "blk", axis=0, tiled=True),
        ),
        query_heads,
        query_frame,
        lookback_heads,
        frame_len,
    )
    newest_max, row_total, accumulated = carry
    attended = (
        (accumulated / row_total[:, :, None])
        .transpose(1, 0, 2)
        .reshape(slab_rows, head_count * DH)
        .astype(jnp.bfloat16)
    )
    tokens_dev = slab_rows // lax.axis_size(("head", "dec"))
    projected = lax.psum_scatter(
        jnp.dot(attended, out_weight, preferred_element_type=jnp.float32).astype(jnp.bfloat16),
        ("head", "dec"),
        scatter_dimension=0,
        tiled=True,
    ).astype(jnp.float32)
    hidden = residual.astype(jnp.float32) + branch_gate[None, :] * projected
    center = jnp.mean(hidden, axis=1, keepdims=True)
    spread = jnp.mean((hidden - center) ** 2, axis=1, keepdims=True)
    normed = (
        (hidden - center) * lax.rsqrt(spread + 1e-06) * (1.0 + final_scale[None, :])
        + final_shift[None, :]
    ).astype(jnp.bfloat16)
    patches = jnp.dot(normed, final_weight, preferred_element_type=jnp.float32).astype(jnp.bfloat16)
    patch_rows = tokens_dev // PW
    tile_rows = 2 * patch_rows
    width = 2 * PW
    tile = (
        patches.reshape(patch_rows, PW, 2, 2, LC)
        .transpose(0, 2, 1, 3, 4)
        .reshape(tile_rows, width * LC)
    )
    padded = padded_2(tile, ((("blk", "head", "dec"), 0),), 1)
    frame_stride = blocks // FRAMES
    frame_index = block_index // frame_stride
    prior_one = from_behind(padded, "blk", frame_stride)
    prior_one = jnp.where(frame_index >= 1, prior_one, padded)
    prior_two = from_behind(prior_one, "blk", frame_stride)
    prior_two = jnp.where(frame_index >= 1, prior_two, padded)
    history = jnp.stack([prior_two, prior_one, padded]).reshape(3, tile_rows + 2, width, LC)
    history = jnp.pad(history, ((0, 0), (0, 0), (1, 1), (0, 0)))
    windows = [
        history[time_tap, row_tap : row_tap + tile_rows, column_tap : column_tap + width, :]
        for time_tap in range(3)
        for row_tap in range(3)
        for column_tap in range(3)
    ]
    columns = jnp.concatenate(windows, axis=-1).reshape(tile_rows * width, 27 * LC)
    summed = (
        jnp.dot(columns, decoder_kernel, preferred_element_type=jnp.float32) + decoder_bias[None, :]
    )
    return summed.astype(jnp.bfloat16).reshape(tile_rows, width, decoder_kernel.shape[1])


def solution(mesh):
    in_specs = (
        P("blk", ("head", "dec")),
        P("blk", ("head", "dec")),
        P("blk", ("head", "dec")),
        P(),
        P(("blk", "head", "dec"), None),
        P(("head", "dec"), None),
        P(),
        P(),
        P(),
        P(),
        P(),
        P(),
    )
    out_specs = P(("blk", "head", "dec"), None, None)
    return jax.shard_map(
        per_device, mesh=mesh, in_specs=in_specs, out_specs=out_specs, check_vma=False
    )
```

profile of v0, /device:TPU:128, one launch (start us, length us, event | category | flops | bytes accessed | tf_op | source)
XLA Modules:
  0.0 315.5 jit_solution(12404184327450962504)
XLA Ops:
  6.5 1.9 copy.25
  9.3 1.1 copy.24
  10.3 0.7 dynamic_slice.3
  11.2 4.4 %broadcast_compare_fusion = pred[256,16384]{1,0:T(8,128)(4,1)} fusion(s32[16384]{0:T(1024)S(1)} %add_select_fusion, s32[256]{0:T(256)S(1)} %and_select_fusion), kind=kLoop, calls=%fused_computation.4 | loop fusion | flops 4194304 | bytes 4260864 | tf_op jit(solution)/shard_map/le | solution.py:49
  15.5 87.7 %all-gather.3.cloned.1.call-done = bf16[16384,384]{0,1:T(8,128)(2,1)} async-done(((bf16[256,384]{0,1:T(8,128)(2,1)}), bf16[16384,384]{0,1:T(8,128)(2,1)}) %all-gather.3.cloned.1.call-update) | async-done | bytes 12582928 | tf_op jit(solution)/shard_map/all_gather | solution.py:94
  103.3 28.9 %select_reduce_fusion = (f32[3,256]{1,0:T(4,128)S(1)}, f32[3,256,16384]{2,1,0:T(8,128)}) fusion(s32[3,256]{1,0:T(4,128)S(1)} %broadcast_subtract_fusion, s32[16384]{0:T(1024)S(1)} %add_select_fusion, pred[256,16384]{1,0:T(8,128)(4,1)} %broadcast_compare_fusion, bf16[256,3,128]{0,2,1:T(8,128)(2,1)S(1)} %bitcast.81, bf16[16384,3,128]{0,2,1:T(8,128)(2,1)} %bitcast.84), kind=kOutput, calls=%fused_computation.2 | convolution fusion | flops 3284139264 | bytes 67377152 | tf_op jit(solution)/shard_map/qhd,khd->hqk/dot_general | solution.py:42
  132.2 25.4 %convert_reduce_fusion = f32[3,256]{1,0:T(4,128)S(1)} fusion(f32[3,256]{1,0:T(4,128)S(1)} %broadcast_maximum_fusion, f32[3,256,16384]{2,1,0:T(8,128)} %get-tuple-element.34, s32[3,256]{1,0:T(4,128)S(1)} %broadcast_subtract_fusion, s32[16384]{0:T(1024)S(1)} %add_select_fusion, pred[256,16384]{1,0:T(8,128)(4,1)} %broadcast_compare_fusion), kind=kLoop, calls=%fused_computation | loop fusion | flops 100662528 | bytes 54600704 | tf_op jit(solution)/shard_map/reduce_sum | solution.py:55
  157.6 38.9 %all-gather.5.cloned.1.call-done = bf16[16384,384]{1,0:T(8,128)(2,1)} async-done(((bf16[256,384]{1,0:T(8,128)(2,1)}), bf16[16384,384]{1,0:T(8,128)(2,1)}) %all-gather.5.cloned.1.call-update) | async-done | bytes 12582928 | tf_op jit(solution)/shard_map/all_gather | solution.py:95
  196.5 16.7 %copy.28 = bf16[16384,384]{0,1:T(8,128)(2,1)} copy(bf16[16384,384]{1,0:T(8,128)(2,1)} %all-gather.5.cloned.1.call-done) | data formatting | bytes 25165824 | tf_op jit(solution)/shard_map/all_gather | solution.py:95
  213.3 24.8 %fusion.2 = bf16[256,3,128]{0,2,1:T(8,128)(2,1)S(1)} fusion(bf16[16384,3,128]{0,2,1:T(8,128)(2,1)} %bitcast.51, f32[256,3]{0,1:T(4,128)S(1)} %bitcast.83, f32[3,256,16384]{2,1,0:T(8,128)} %get-tuple-element.34, f32[3,256]{1,0:T(4,128)S(1)} %broadcast_maximum_fusion, s32[3,256]{1,0:T(4,128)S(1)} %broadcast_subtract_fusion, s32[16384]{0:T(1024)S(1)} %add_select_fusion, ...), kind=kOutput, calls=%fused_computation.10 | convolution fusion | flops 3296919552 | bytes 67380224 | tf_op jit(solution)/shard_map/hqk,khd->hqd/dot_general | solution.py:56
  238.1 2.2 convolution_convert_fusion
  240.3 28.1 %reduce-scatter.2.cloned.1.call-done = bf16[64,3072]{1,0:T(8,128)(2,1)} async-done(((bf16[256,3072]{1,0:T(8,128)(2,1)}), bf16[64,3072]{1,0:T(8,128)(2,1)}) %reduce-scatter.2.cloned.1.call-update) | async-done | bytes 393232 | tf_op jit(solution)/shard_map/reduce_scatter | solution.py:110
  268.4 1.2 fusion.3
  269.7 1.3 multiply_reduce_fusion
  271.0 1.4 convolution_convert_fusion.1
  272.8 2.2 collective-permute-start
  275.1 8.7 %collective-permute-start.1 = (bf16[1,1024]{1,0:T(2,128)(2,1)S(1)}, bf16[1,1024]{1,0:T(2,128)(2,1)S(1)}, u32[]{:S(2)}, u32[]{:S(2)}) collective-permute-start(bf16[1,1024]{1,0:T(2,128)(2,1)S(1)} %get-tuple-element.32), channel_id=1, source_target_pairs={{1,0},{2,1},{3,2},{4,3},{5,4},{6,5},{7,6},{8,7},{9,8},{10,9},{11,1... | collective-permute-start | bytes 6152 | tf_op jit(solution)/shard_map/ppermute | solution.py:22
  284.1 1.0 collective-permute-done.1
  285.4 1.9 collective-permute-start.2
  287.5 4.7 %collective-permute-done.2 = bf16[6,1024]{1,0:T(8,128)(2,1)S(1)} collective-permute-done((bf16[6,1024]{1,0:T(8,128)(2,1)S(1)}, bf16[6,1024]{1,0:T(8,128)(2,1)S(1)}, u32[]{:S(2)}, u32[]{:S(2)}) %collective-permute-start.2) | collective-permute-done | bytes 12320 | tf_op jit(solution)/shard_map/ppermute | solution.py:32
  292.2 1.9 collective-permute-start.3
  295.1 4.0 %collective-permute-done.3 = bf16[6,1024]{1,0:T(8,128)(2,1)S(1)} collective-permute-done((bf16[6,1024]{1,0:T(8,128)(2,1)S(1)}, bf16[6,1024]{1,0:T(8,128)(2,1)S(1)}, u32[]{:S(2)}, u32[]{:S(2)}) %collective-permute-start.3) | collective-permute-done | bytes 12320 | tf_op jit(solution)/shard_map/ppermute | solution.py:32
  304.7 2.2 concatenate.111
  306.9 2.1 fusion
  (70 shorter events, 8.5 us)
Async XLA Ops:
  6.5 231.6 %copy-start = (bf16[384,3072]{1,0:T(8,128)(2,1)S(1)}, bf16[384,3072]{1,0:T(8,128)(2,1)}, u32[]{:S(2)}) copy-start(bf16[384,3072]{1,0:T(8,128)(2,1)} %param.17) | copy-start | bytes 7077892
  6.5 96.7 %all-gather.3.cloned.1.call-start = ((), (), s32[]{:S(2)}) async-start(), calls=%async_computation.1 | async-start | bytes 12779520 | tf_op jit(solution)/shard_map/all_gather | solution.py:94
  8.5 188.1 %all-gather.5.cloned.1.call-start = ((), (), s32[]{:S(2)}) async-start(), calls=%async_computation.2 | async-start | bytes 12779520 | tf_op jit(solution)/shard_map/all_gather | solution.py:95
  9.2 259.2 %reduce-scatter.2.cloned.1.call-start = ((), (), s32[]{:S(2)}) async-start(), calls=%async_computation.3 | async-start | bytes 1966080 | tf_op jit(solution)/shard_map/reduce_scatter | solution.py:110
  213.2 27.1 %copy-start.3 = (f32[3072]{0:T(1024)S(1)}, f32[3072]{0:T(1024)}, u32[]{:S(2)}) copy-start(f32[3072]{0:T(1024)} %param.20) | copy-start | bytes 36868
  213.2 55.2 %copy-start.1 = (bf16[64,3072]{1,0:T(8,128)(2,1)S(1)}, bf16[64,3072]{1,0:T(8,128)(2,1)}, u32[]{:S(2)}) copy-start(bf16[64,3072]{1,0:T(8,128)(2,1)} %param.16) | copy-start | bytes 1179652
  213.2 55.2 %copy-start.2 = (f32[3072]{0:T(1024)S(1)}, f32[3072]{0:T(1024)}, u32[]{:S(2)}) copy-start(f32[3072]{0:T(1024)} %param.18) | copy-start | bytes 36868
  213.2 57.7 %copy-start.4 = (bf16[3072,64]{0,1:T(8,128)(2,1)S(1)}, bf16[3072,64]{0,1:T(8,128)(2,1)}, u32[]{:S(2)}) copy-start(bf16[3072,64]{0,1:T(8,128)(2,1)} %param.21) | copy-start | bytes 1179652
  213.2 57.7 %copy-start.5 = (f32[3072]{0:T(1024)S(1)}, f32[3072]{0:T(1024)}, u32[]{:S(2)}) copy-start(f32[3072]{0:T(1024)} %param.19) | copy-start | bytes 36868
  272.8 11.1 %collective-permute-start = (bf16[1,1024]{1,0:T(2,128)(2,1)S(1)}, bf16[1,1024]{1,0:T(2,128)(2,1)S(1)}, u32[]{:S(2)}, u32[]{:S(2)}) collective-permute-start(bf16[1,1024]{1,0:T(2,128)(2,1)S(1)} %get-tuple-element.31), channel_id=1, source_target_pairs={{0,1},{1,2},{2,3},{3,4},{4,5},{5,6},{6,7},{7,8},{8,9},{9,10},{10,1... | collective-permute-start | bytes 6152 | tf_op jit(solution)/shard_map/ppermute | solution.py:20
  275.1 10.1 %collective-permute-start.1 = (bf16[1,1024]{1,0:T(2,128)(2,1)S(1)}, bf16[1,1024]{1,0:T(2,128)(2,1)S(1)}, u32[]{:S(2)}, u32[]{:S(2)}) collective-permute-start(bf16[1,1024]{1,0:T(2,128)(2,1)S(1)} %get-tuple-element.32), channel_id=1, source_target_pairs={{1,0},{2,1},{3,2},{4,3},{5,4},{6,5},{7,6},{8,7},{9,8},{10,9},{11,1... | collective-permute-start | bytes 6152 | tf_op jit(solution)/shard_map/ppermute | solution.py:22
  285.4 6.8 %collective-permute-start.2 = (bf16[6,1024]{1,0:T(8,128)(2,1)S(1)}, bf16[6,1024]{1,0:T(8,128)(2,1)S(1)}, u32[]{:S(2)}, u32[]{:S(2)}) collective-permute-start(bf16[6,1024]{1,0:T(8,128)(2,1)S(1)} %pad_maximum_fusion.2), channel_id=1, source_target_pairs={{0,32},{4,36},{8,40},{12,44},{16,48},{20,52},{24,56},{28,60},{32,6... | collective-permute-start | bytes 36872 | tf_op jit(solution)/shard_map/ppermute | solution.py:32
  292.2 6.8 %collective-permute-start.3 = (bf16[6,1024]{1,0:T(8,128)(2,1)S(1)}, bf16[6,1024]{1,0:T(8,128)(2,1)S(1)}, u32[]{:S(2)}, u32[]{:S(2)}) collective-permute-start(bf16[6,1024]{1,0:T(8,128)(2,1)S(1)} %broadcast_select_fusion.1), channel_id=1, source_target_pairs={{0,32},{4,36},{8,40},{12,44},{16,48},{20,52},{24,56},{28,60},{32,6... | collective-permute-start | bytes 36872 | tf_op jit(solution)/shard_map/ppermute | solution.py:32
Sparse Core Ops, SparseCore 0:
  10.0 93.2 all-gather.2
  106.0 90.4 all-gather.4
  240.4 27.9 reduce-scatter.1
where the time goes:
time: 316 us
  waiting for transfers between devices  165 us (52%)
  matrix products  59.4 us (19%)
  other arithmetic  32.6 us (10%)
  local copies, waits for them, and re-layouts  30 us (9%)
  starting transfers between devices  14.9 us (5%)
  between operations  13.4 us (4%)
    all_gather x1, waiting for transfers between devices, per_device(): lax.all_gather(key_vectors, 'blk', axis=0, tiled=True)  87.7 us
    all_gather x1, waiting for transfers between devices, per_device(): lax.all_gather(values, 'blk', axis=0, tiled=True)  38.9 us
    dot_general x1, matrix products, attend_block(): jnp.einsum('qhd,khd->hqk', query_heads, key_heads, preferred_element_type...  28.9 us
    reduce_scatter x1, waiting for transfers between devices, per_device(): lax.psum_scatter(jnp.dot(attended, out_weight, preferred_element_type=jnp...  28.1 us
    reduce_sum x1, other arithmetic, attend_block(): row_total = jnp.sum(weights.astype(jnp.float32), axis=2)  25.4 us
    dot_general x1, matrix products, attend_block(): jnp.einsum('hqk,khd->hqd', weights, value_heads, preferred_element_type=j...  24.8 us
    all_gather x1, local copies, waits for them, and re-layouts, per_device(): lax.all_gather(values, 'blk', axis=0, tiled=True)  16.7 us
    ppermute x1, starting transfers between devices, padded_2(): lax.ppermute(head, axis, [((i + 1) % count, i) for i in range(ends)])  8.75 us
  transfers between devices with their start and end apart: 7, of which 6 were waited for; matrix products, arithmetic and copies ran while one was open for 20% of the time, Pallas kernels for 0%

commit v1 on v0

--- a/solution.py
+++ b/solution.py
@@ -91,7 +91,9 @@
     carry = attend_block(
         initial,
         (
-            lax.all_gather(key_vectors, "blk", axis=0, tiled=True),
+            jnp.concatenate(
+                lax.all_to_all(jnp.stack([key_vectors] * lax.axis_size("blk")), "blk", 0, 0), axis=0
+            ),
             lax.all_gather(values, "blk", axis=0, tiled=True),
         ),
         query_heads,

time: 316 us -> 545 us (1.72)
  waiting for transfers between devices: 165 us -> 346 us
  local copies, waits for them, and re-layouts: 30 us -> 66.2 us
  starting transfers between devices: 14.9 us -> 25.4 us
    all_to_all x0 -> x1, waiting for transfers between devices: none -> 304 us  [per_device(): lax.all_to_all(jnp.stack([key_vectors] * lax.axis_size('blk')), 'blk', 0, 0)]
    all_gather x1 -> x0, waiting for transfers between devices: 87.7 us -> none  [per_device(): lax.all_gather(key_vectors, 'blk', axis=0, tiled=True)]
    all_gather x1, waiting for transfers between devices: 38.9 us -> 0.02 us  [per_device(): lax.all_gather(values, 'blk', axis=0, tiled=True)]
    another operation x0 -> x2, local copies, waits for them, and re-layouts: none -> 25.6 us  [the longest x1 19.6 us: attend_block(): key_heads = key_block.reshape(key_count, head_count, DH)]
    all_to_all x0 -> x1, local copies, waits for them, and re-layouts: none -> 14 us  [per_device(): lax.all_to_all(jnp.stack([key_vectors] * lax.axis_size('blk')), 'blk', 0, 0)]
    all_to_all x0 -> x1, starting transfers between devices: none -> 10.5 us  [per_device(): lax.all_to_all(jnp.stack([key_vectors] * lax.axis_size('blk')), 'blk', 0, 0)]
  transfers between devices with their start and end apart: 7 -> 7, of which waited for: 6 -> 5; matrix products, arithmetic and copies ran while one was open for 20% -> 17% of each run, Pallas kernels for 0% -> 0%
where the time goes in v1:
time: 545 us; the launch traced here: 544 us
  waiting for transfers between devices  346 us (63%)
  local copies, waits for them, and re-layouts  66.2 us (12%)
  matrix products  59.5 us (11%)
  other arithmetic  32.6 us (6%)
  starting transfers between devices  25.4 us (5%)
  between operations  13.7 us (3%)
    all_to_all x1, waiting for transfers between devices, per_device(): lax.all_to_all(jnp.stack([key_vectors] * lax.axis_size('blk')), 'blk', 0, 0)  304 us
    reduce_scatter x1, waiting for transfers between devices, per_device(): lax.psum_scatter(jnp.dot(attended, out_weight, preferred_element_type=jnp...  32.4 us
    dot_general x1, matrix products, attend_block(): jnp.einsum('qhd,khd->hqk', query_heads, key_heads, preferred_element_type...  28.9 us
    reduce_sum x1, other arithmetic, attend_block(): row_total = jnp.sum(weights.astype(jnp.float32), axis=2)  25.4 us
    dot_general x1, matrix products, attend_block(): jnp.einsum('hqk,khd->hqd', weights, value_heads, preferred_element_type=j...  24.9 us
    another operation x1, local copies, waits for them, and re-layouts, attend_block(): key_heads = key_block.reshape(key_count, head_count, DH)  19.6 us
    all_gather x1, local copies, waits for them, and re-layouts, per_device(): lax.all_gather(values, 'blk', axis=0, tiled=True)  15.6 us
    all_to_all x1, local copies, waits for them, and re-layouts, per_device(): lax.all_to_all(jnp.stack([key_vectors] * lax.axis_size('blk')), 'blk', 0, 0)  14 us
  transfers between devices with their start and end apart: 7, of which 5 were waited for; matrix products, arithmetic and copies ran while one was open for 17% of the time, Pallas kernels for 0%

profile of v1, /device:TPU:128, one launch (start us, length us, event | category | flops | bytes accessed | tf_op | source)
XLA Modules:
  0.0 543.8 jit_solution(362755646300982176)
XLA Ops:
  6.5 1.2 copy.25
  7.8 6.0 %stack.8 = bf16[64,256,384]{1,2,0:T(8,128)(2,1)} broadcast(bf16[256,384]{0,1:T(8,128)(2,1)S(1)} %copy.25), dimensions={1,2} | broadcast | bytes 12779520 | tf_op jit(solution)/shard_map/stack | solution.py:95
  13.8 10.5 %all-to-all-start = ((bf16[64,256,384]{1,2,0:T(8,128)(2,1)}), bf16[64,256,384]{1,2,0:T(8,128)(2,1)}, u32[]{:S(2)}, u32[]{:S(2)}) async-start(bf16[64,256,384]{1,2,0:T(8,128)(2,1)} %stack.8), calls=%async_computation | async-start | bytes 25165824 | tf_op jit(solution)/shard_map/all_to_all | solution.py:95
  25.4 4.4 broadcast_compare_fusion
  29.8 303.5 %all-to-all-done = bf16[64,256,384]{1,2,0:T(8,128)(2,1)} async-done(((bf16[64,256,384]{1,2,0:T(8,128)(2,1)}), bf16[64,256,384]{1,2,0:T(8,128)(2,1)}, u32[]{:S(2)}, u32[]{:S(2)}) %all-to-all-start) | async-done | bytes 12582944 | tf_op jit(solution)/shard_map/all_to_all | solution.py:95
  333.3 14.0 %copy.26 = bf16[64,256,384]{1,0,2:T(8,128)(2,1)} copy(bf16[64,256,384]{1,2,0:T(8,128)(2,1)} %all-to-all-done) | data formatting | bytes 25165824 | tf_op jit(solution)/shard_map/all_to_all | solution.py:95
  347.3 19.6 %reshape_reshape.3 = bf16[16384,3,128]{0,2,1:T(8,128)(2,1)} reshape(bf16[64,256,384]{1,0,2:T(8,128)(2,1)} %copy.26) | data formatting | bytes 25165824 | tf_op jit(solution)/shard_map/reshape;reshape | solution.py:40
  366.8 28.9 %select_reduce_fusion = (f32[3,256]{1,0:T(4,128)S(1)}, f32[3,256,16384]{2,1,0:T(8,128)}) fusion(s32[3,256]{1,0:T(4,128)S(1)} %broadcast_subtract_fusion, s32[16384]{0:T(1024)S(1)} %add_select_fusion, pred[256,16384]{1,0:T(8,128)(4,1)} %broadcast_compare_fusion, bf16[256,3,128]{0,2,1:T(8,128)(2,1)S(1)} %bitcast.82, bf16[16384,3,128]{0,2,1:T(8,128)(2,1)} %reshape_reshape.3), kind=kOutput, calls=%fused_computation.2 | convolution fusion | flops 3284139264 | bytes 67377152 | tf_op jit(solution)/shard_map/qhd,khd->hqk/dot_general | solution.py:42
  395.8 25.4 %convert_reduce_fusion = f32[3,256]{1,0:T(4,128)S(1)} fusion(f32[3,256]{1,0:T(4,128)S(1)} %broadcast_maximum_fusion, f32[3,256,16384]{2,1,0:T(8,128)} %get-tuple-element.34, s32[3,256]{1,0:T(4,128)S(1)} %broadcast_subtract_fusion, s32[16384]{0:T(1024)S(1)} %add_select_fusion, pred[256,16384]{1,0:T(8,128)(4,1)} %broadcast_compare_fusion), kind=kLoop, calls=%fused_computation | loop fusion | flops 100662528 | bytes 54600704 | tf_op jit(solution)/shard_map/reduce_sum | solution.py:55
  421.2 15.6 %copy.29 = bf16[16384,384]{0,1:T(8,128)(2,1)} copy(bf16[16384,384]{1,0:T(8,128)(2,1)} %all-gather.2.cloned.1.call-done) | data formatting | bytes 25165824 | tf_op jit(solution)/shard_map/all_gather | solution.py:97
  436.8 24.9 %fusion.2 = bf16[256,3,128]{0,2,1:T(8,128)(2,1)S(1)} fusion(bf16[16384,3,128]{0,2,1:T(8,128)(2,1)} %bitcast.52, f32[256,3]{0,1:T(4,128)S(1)} %bitcast.84, f32[3,256,16384]{2,1,0:T(8,128)} %get-tuple-element.34, f32[3,256]{1,0:T(4,128)S(1)} %broadcast_maximum_fusion, s32[3,256]{1,0:T(4,128)S(1)} %broadcast_subtract_fusion, s32[16384]{0:T(1024)S(1)} %add_select_fusion, ...), kind=kOutput, calls=%fused_computation.10 | convolution fusion | flops 3296919552 | bytes 67380224 | tf_op jit(solution)/shard_map/hqk,khd->hqd/dot_general | solution.py:56
  461.8 2.2 convolution_convert_fusion
  464.0 32.4 %reduce-scatter.2.cloned.1.call-done = bf16[64,3072]{1,0:T(8,128)(2,1)} async-done(((bf16[256,3072]{1,0:T(8,128)(2,1)}), bf16[64,3072]{1,0:T(8,128)(2,1)}) %reduce-scatter.2.cloned.1.call-update) | async-done | bytes 393232 | tf_op jit(solution)/shard_map/reduce_scatter | solution.py:112
  496.4 1.2 fusion.3
  497.6 1.3 multiply_reduce_fusion
  499.0 1.4 convolution_convert_fusion.1
  500.8 2.3 collective-permute-start
  503.1 8.7 %collective-permute-start.1 = (bf16[1,1024]{1,0:T(2,128)(2,1)S(1)}, bf16[1,1024]{1,0:T(2,128)(2,1)S(1)}, u32[]{:S(2)}, u32[]{:S(2)}) collective-permute-start(bf16[1,1024]{1,0:T(2,128)(2,1)S(1)} %get-tuple-element.32), channel_id=1, source_target_pairs={{1,0},{2,1},{3,2},{4,3},{5,4},{6,5},{7,6},{8,7},{9,8},{10,9},{11,1... | collective-permute-start | bytes 6152 | tf_op jit(solution)/shard_map/ppermute | solution.py:22
  513.3 1.9 collective-permute-start.2
  515.5 4.7 collective-permute-done.2
  520.2 1.9 collective-permute-start.3
  523.1 4.0 collective-permute-done.3
  532.6 2.2 concatenate.111
  534.8 2.1 fusion
  (76 shorter events, 9.7 us)
Async XLA Ops:
  6.5 455.2 %copy-start = (bf16[384,3072]{1,0:T(8,128)(2,1)S(1)}, bf16[384,3072]{1,0:T(8,128)(2,1)}, u32[]{:S(2)}) copy-start(bf16[384,3072]{1,0:T(8,128)(2,1)} %param.17) | copy-start | bytes 7077892
  7.8 17.3 %copy-start.2 = (bf16[256,384]{1,0:T(8,128)(2,1)S(1)}, bf16[256,384]{1,0:T(8,128)(2,1)}, u32[]{:S(2)}) copy-start(bf16[256,384]{1,0:T(8,128)(2,1)} %param.12) | copy-start | bytes 589828
  7.8 17.5 %copy-start.7 = (s32[12]{0:T(128)S(1)}, s32[12]{0:T(128)}, u32[]{:S(2)}) copy-start(s32[12]{0:T(128)} %param.15) | copy-start | bytes 148
  13.8 319.5 %all-to-all-start = ((bf16[64,256,384]{1,2,0:T(8,128)(2,1)}), bf16[64,256,384]{1,2,0:T(8,128)(2,1)}, u32[]{:S(2)}, u32[]{:S(2)}) async-start(bf16[64,256,384]{1,2,0:T(8,128)(2,1)} %stack.8), calls=%async_computation | async-start | bytes 25165824 | tf_op jit(solution)/shard_map/all_to_all | solution.py:95
  24.3 396.9 %all-gather.2.cloned.1.call-start = ((), (), s32[]{:S(2)}) async-start(), calls=%async_computation.2 | async-start | bytes 12779520 | tf_op jit(solution)/shard_map/all_gather | solution.py:97
  25.0 471.4 %reduce-scatter.2.cloned.1.call-start = ((), (), s32[]{:S(2)}) async-start(), calls=%async_computation.3 | async-start | bytes 1966080 | tf_op jit(solution)/shard_map/reduce_scatter | solution.py:112
  436.8 27.2 %copy-start.4 = (f32[3072]{0:T(1024)S(1)}, f32[3072]{0:T(1024)}, u32[]{:S(2)}) copy-start(f32[3072]{0:T(1024)} %param.20) | copy-start | bytes 36868
  436.8 59.6 %copy-start.1 = (bf16[64,3072]{1,0:T(8,128)(2,1)S(1)}, bf16[64,3072]{1,0:T(8,128)(2,1)}, u32[]{:S(2)}) copy-start(bf16[64,3072]{1,0:T(8,128)(2,1)} %param.16) | copy-start | bytes 1179652
  436.8 59.6 %copy-start.3 = (f32[3072]{0:T(1024)S(1)}, f32[3072]{0:T(1024)}, u32[]{:S(2)}) copy-start(f32[3072]{0:T(1024)} %param.18) | copy-start | bytes 36868
  436.8 62.1 %copy-start.5 = (bf16[3072,64]{0,1:T(8,128)(2,1)S(1)}, bf16[3072,64]{0,1:T(8,128)(2,1)}, u32[]{:S(2)}) copy-start(bf16[3072,64]{0,1:T(8,128)(2,1)} %param.21) | copy-start | bytes 1179652
  436.8 62.1 %copy-start.6 = (f32[3072]{0:T(1024)S(1)}, f32[3072]{0:T(1024)}, u32[]{:S(2)}) copy-start(f32[3072]{0:T(1024)} %param.19) | copy-start | bytes 36868
  500.8 11.1 %collective-permute-start = (bf16[1,1024]{1,0:T(2,128)(2,1)S(1)}, bf16[1,1024]{1,0:T(2,128)(2,1)S(1)}, u32[]{:S(2)}, u32[]{:S(2)}) collective-permute-start(bf16[1,1024]{1,0:T(2,128)(2,1)S(1)} %get-tuple-element.31), channel_id=1, source_target_pairs={{0,1},{1,2},{2,3},{3,4},{4,5},{5,6},{6,7},{7,8},{8,9},{9,10},{10,1... | collective-permute-start | bytes 6152 | tf_op jit(solution)/shard_map/ppermute | solution.py:20
  503.1 10.1 %collective-permute-start.1 = (bf16[1,1024]{1,0:T(2,128)(2,1)S(1)}, bf16[1,1024]{1,0:T(2,128)(2,1)S(1)}, u32[]{:S(2)}, u32[]{:S(2)}) collective-permute-start(bf16[1,1024]{1,0:T(2,128)(2,1)S(1)} %get-tuple-element.32), channel_id=1, source_target_pairs={{1,0},{2,1},{3,2},{4,3},{5,4},{6,5},{7,6},{8,7},{9,8},{10,9},{11,1... | collective-permute-start | bytes 6152 | tf_op jit(solution)/shard_map/ppermute | solution.py:22
  513.3 6.8 %collective-permute-start.2 = (bf16[6,1024]{1,0:T(8,128)(2,1)S(1)}, bf16[6,1024]{1,0:T(8,128)(2,1)S(1)}, u32[]{:S(2)}, u32[]{:S(2)}) collective-permute-start(bf16[6,1024]{1,0:T(8,128)(2,1)S(1)} %pad_maximum_fusion.2), channel_id=1, source_target_pairs={{0,32},{4,36},{8,40},{12,44},{16,48},{20,52},{24,56},{28,60},{32,6... | collective-permute-start | bytes 36872 | tf_op jit(solution)/shard_map/ppermute | solution.py:32
  520.2 6.8 %collective-permute-start.3 = (bf16[6,1024]{1,0:T(8,128)(2,1)S(1)}, bf16[6,1024]{1,0:T(8,128)(2,1)S(1)}, u32[]{:S(2)}, u32[]{:S(2)}) collective-permute-start(bf16[6,1024]{1,0:T(8,128)(2,1)S(1)} %broadcast_select_fusion.1), channel_id=1, source_target_pairs={{0,32},{4,36},{8,40},{12,44},{16,48},{20,52},{24,56},{28,60},{32,6... | collective-permute-start | bytes 36872 | tf_op jit(solution)/shard_map/ppermute | solution.py:32
Sparse Core Ops, SparseCore 0:
  27.8 204.4 all-gather.1
  464.1 32.2 reduce-scatter.1
